TPU v7x, 512 devices: a whole 4x8x8 slice. The times are simulated.
512 devices in a mesh: freq: 16 (over y, core), trace: 32 (over z, x).
Axes of the slice: x: 4, y: 8, z: 8, core: 2. Of those that a mesh axis runs over, the one named last changes fastest.
Arguments:
- traces: bfloat16 [64, 128, 2048], P('trace', 'freq'), may hold values from -20 to 20
- omega: float32 [2, 33, 64, 64], replicated, may hold values from -0.125 to 0.125
Outputs:
- denoised: float32 [64, 128, 2048], P('trace', 'freq')
All inputs are finite; a program needn't handle non-finite values.
Results may differ from a plain program's by a relative error of at most 0.0003.
Values sent between devices are 32-bit elements; how exact they have to be, the bound alone decides.
No kernel may reach another device: no remote copies, remote signals or barrier semaphores. Data moves between devices by JAX's collectives and lax.ppermute only.
A program may use at most 64 MiB of HBM per device.

v0:
```python
import math
import jax
import jax.numpy as jnp
from jax import lax
from jax.sharding import PartitionSpec as P

FREQ_DEV = 1
highest = lax.Precision.HIGHEST


def fourier_tables(samples, freq_total):
    moments = jnp.arange(samples, dtype=jnp.int32)
    bins = jnp.arange(freq_total, dtype=jnp.int32) + 1
    phases = bins[:, None] * moments[None, :] % samples
    angles = phases.astype(jnp.float32) * (2.0 * math.pi / samples)
    return (jnp.cos(angles), jnp.sin(angles))


def anti_counts(spots, length, window, lags):
    counted = jnp.minimum(jnp.minimum(spots + 1, length - spots), min(window, lags))
    return counted.astype(jnp.float32)


def solve_one(factor, right_side):
    return jax.scipy.linalg.cho_solve((factor, True), right_side)


def body(traces, omega):
    rows_dev, cols_dev, samples = traces.shape
    lag_x, lag_y, rank_size = (omega.shape[1], omega.shape[2], omega.shape[3])
    trace_count = lax.axis_size("trace")
    freq_count = lax.axis_size("freq")
    patch_x = rows_dev * trace_count
    patch_y = cols_dev * freq_count
    win_x = patch_x - lag_x + 1
    win_y = patch_y - lag_y + 1
    freq_total = FREQ_DEV * freq_count
    own_rows = win_x // trace_count
    own_lags = lag_y // trace_count
    position = lax.axis_index("trace")
    cosine_table, sine_table = fourier_tables(samples, freq_total)
    norm_scale = 1.0 / math.sqrt(samples)
    forward = jnp.stack([cosine_table.T, -sine_table.T], axis=1) * norm_scale
    spectrum = jnp.einsum("xyt,tpk->xypk", traces.astype(jnp.float32), forward, precision=highest)
    spectrum = lax.all_to_all(spectrum, "freq", split_axis=3, concat_axis=1, tiled=True)
    slices = jnp.transpose(spectrum, (3, 2, 0, 1))
    whole_slices = lax.all_gather(slices, "trace", axis=2, tiled=True)
    freq_dev = whole_slices.shape[0]
    first_row = position * own_rows
    row_slabs = jnp.stack([lax.dynamic_slice_in_dim(whole_slices, first_row + 0, lag_x, 2)], axis=1)
    hankel = jnp.stack([row_slabs[..., anchor : anchor + lag_y] for anchor in range(win_y)], axis=3)
    hankel_flat = hankel.reshape(freq_dev, own_rows * 2 * win_y, lag_x * lag_y)
    omega_flat = omega.reshape(2, lag_x * lag_y, rank_size)
    products = jnp.einsum("fnm,smq->fnsq", hankel_flat, omega_flat, precision=highest)
    products = products.reshape(freq_dev, own_rows, 2, win_y, 2, rank_size)
    sketch_re = products[:, :, 0, :, 0] - products[:, :, 1, :, 1]
    sketch_im = products[:, :, 0, :, 1] + products[:, :, 1, :, 0]
    own_sketch = jnp.transpose(jnp.concatenate([sketch_re, sketch_im], -1), (1, 0, 2, 3))
    sketch = lax.all_gather(own_sketch, "trace", axis=0, tiled=True)
    inner = lax.psum(
        jnp.einsum("afbp,afbq->fpq", own_sketch, own_sketch, precision=highest), "trace"
    )
    lag_start = position * own_lags
    hankel_blocks = []
    for offset in range(own_lags):
        band = lax.dynamic_slice_in_dim(whole_slices, lag_start + offset, win_y, 3)
        hankel_blocks.append(
            jnp.stack([band[:, :, anchor : anchor + win_x] for anchor in range(lag_x)], axis=2)
        )
    columns = jnp.stack(hankel_blocks, axis=1).reshape(
        freq_dev, own_lags * 2 * lag_x, win_x * win_y
    )
    flat_sketch = jnp.transpose(sketch, (1, 0, 2, 3)).reshape(
        freq_dev, win_x * win_y, 2 * rank_size
    )
    project = jnp.einsum("fnm,fmq->fnq", columns, flat_sketch, precision=highest).reshape(
        freq_dev, own_lags, 2, lag_x, 2 * rank_size
    )
    proj_re = jnp.transpose(
        project[:, :, 0, :, :rank_size] + project[:, :, 1, :, rank_size:], (0, 3, 1, 2)
    )
    proj_im = jnp.transpose(
        project[:, :, 1, :, :rank_size] - project[:, :, 0, :, rank_size:], (0, 3, 1, 2)
    )
    gram_re = inner[:, :rank_size, :rank_size] + inner[:, rank_size:, rank_size:]
    gram_im = inner[:, :rank_size, rank_size:] - inner[:, rank_size:, :rank_size]
    real_gram = jnp.concatenate(
        [jnp.concatenate([gram_re, -gram_im], 2), jnp.concatenate([gram_im, gram_re], 2)], 1
    )
    right_side = jnp.concatenate([proj_re, proj_im], 1).reshape(
        freq_dev, 2 * rank_size, own_lags * lag_x
    )
    factor = jnp.linalg.cholesky(real_gram)
    solved = jax.vmap(solve_one)(factor, right_side)
    mix_re = solved[:, :rank_size]
    mix_im = solved[:, rank_size:]
    mix_real = jnp.concatenate([mix_re, -mix_im], 1).reshape(
        freq_dev, 2 * rank_size, own_lags, lag_x
    )
    mix_imag = jnp.concatenate([mix_im, mix_re], 1).reshape(
        freq_dev, 2 * rank_size, own_lags, lag_x
    )
    mixing = jnp.stack([mix_real, mix_imag], axis=3)
    sketch_cols = jnp.transpose(sketch, (1, 2, 3, 0))
    lowrank = jnp.einsum("fqezc,fbqa->fbezca", mixing, sketch_cols, precision=highest)
    target = (
        jnp.arange(lag_x, dtype=jnp.int32)[:, None] + jnp.arange(win_x, dtype=jnp.int32)[None, :]
    ).reshape(-1)
    diagonal = (target[:, None] == jnp.arange(patch_x, dtype=jnp.int32)[None, :]).astype(
        jnp.float32
    )
    spread = jnp.dot(lowrank.reshape(-1, lag_x * win_x), diagonal, precision=highest).reshape(
        freq_dev, win_y, own_lags, 2, patch_x
    )
    partial_value = jnp.zeros((patch_x, freq_dev, 2, patch_y), jnp.float32)
    zero_index = jnp.zeros((), jnp.int32)
    for offset in range(own_lags):
        band_block = jnp.transpose(spread[:, :, offset], (3, 0, 2, 1))
        partial_value = partial_value + lax.dynamic_update_slice(
            jnp.zeros_like(partial_value),
            band_block,
            (zero_index, zero_index, zero_index, lag_start + offset),
        )
    averaged = lax.psum_scatter(partial_value, "trace", scatter_dimension=0, tiled=True)
    spots_x = position * rows_dev + jnp.arange(rows_dev, dtype=jnp.int32)
    spots_y = jnp.arange(patch_y, dtype=jnp.int32)
    counts = (
        anti_counts(spots_x, patch_x, win_x, lag_x)[:, None, None, None]
        * anti_counts(spots_y, patch_y, win_y, lag_y)[None, None, None, :]
    )
    averaged = averaged / counts
    returned = lax.all_to_all(averaged, "freq", split_axis=3, concat_axis=1, tiled=True)
    inverse = jnp.stack([cosine_table, -sine_table], axis=1) * (2.0 * norm_scale)
    return jnp.einsum("xkpy,kpt->xyt", returned, inverse, precision=highest)


def solution(mesh):
    return jax.shard_map(
        body,
        mesh=mesh,
        in_specs=(P("trace", "freq", None), P()),
        out_specs=P("trace", "freq", None),
        check_vma=False,
    )
```

profile of v0, /device:TPU:1, one launch (start us, length us, event | category | flops | bytes accessed | tf_op | source)
XLA Modules:
  0.0 583.4 jit_solution(9340026111584924302)
XLA Ops:
  7.2 1.4 convolution_bitcast_fusion.5
  9.3 10.1 %all-to-all-start = ((f32[2,8,2,16]{1,0,2,3:T(2,128)}), f32[2,8,2,16]{1,0,2,3:T(2,128)S(1)}, u32[]{:S(2)}, u32[]{:S(2)}) async-start(f32[2,8,2,16]{1,0,2,3:T(2,128)} %copy.367), calls=%async_computation | async-start | bytes 65536 | tf_op jit(solution)/shard_map/all_to_all | solution.py:45
  19.5 7.4 %all-to-all-done = f32[2,8,2,16]{1,0,2,3:T(2,128)S(1)} async-done(((f32[2,8,2,16]{1,0,2,3:T(2,128)}), f32[2,8,2,16]{1,0,2,3:T(2,128)S(1)}, u32[]{:S(2)}, u32[]{:S(2)}) %all-to-all-start) | async-done | bytes 2080 | tf_op jit(solution)/shard_map/all_to_all | solution.py:45
  27.0 41.2 %all_gather.6 = f32[1,2,64,128]{3,1,0,2:T(2,128)S(1)} all-gather(f32[1,2,2,128]{3,1,0,2:T(2,128)S(1)} %bitcast.277), channel_id=1, replica_groups=mesh['freq'=16,'trace'=32] {'trace'}, dimensions={2}, use_global_device_ids=true | all-gather | bytes 67584 | tf_op jit(solution)/shard_map/all_gather | solution.py:47
  68.2 1.6 fusion.69
  69.8 1.4 fusion.68
  71.9 1.0 fusion.70
  73.0 0.8 copy.379
  74.4 0.8 copy.380
  75.9 0.8 copy.381
  77.3 0.8 copy.382
  78.8 0.8 copy.383
  80.2 0.8 copy.384
  81.7 0.8 copy.385
  83.1 0.8 copy.386
  84.6 0.8 copy.387
  86.0 0.8 copy.388
  87.5 0.8 copy.389
  88.9 0.8 copy.390
  90.4 0.8 copy.391
  91.8 0.8 copy.392
  93.3 0.8 copy.393
  94.7 0.8 copy.394
  96.2 0.8 copy.395
  97.6 0.8 copy.396
  99.1 0.8 copy.397
  133.9 9.0 %stack.490 = f32[2,65,2112]{2,1,0:T(8,128)S(1)} concatenate(f32[2,1,2112]{2,1,0:T(1,128)} %stack.562, f32[2,1,2112]{2,1,0:T(1,128)} %stack.563, f32[2,1,2112]{2,1,0:T(1,128)} %stack.564, f32[2,1,2112]{2,1,0:T(1,128)} %stack.565, f32[2,1,2112]{2,1,0:T(1,128)} %stack.566, f32[2,1,2112]{2,1,0:T(1,128)} %stack.567, f32[2,1,2112]{2,1,0:T(1,128)} %stack.568, f32[2,1,2112]{2,1,0:T(1,128)} %stack.569, ...), dimensions={1} | concatenate | bytes 2196480 | tf_op jit(solution)/shard_map/stack | solution.py:51
  142.9 3.6 fusion.6
  146.6 0.9 convolution_bitcast_fusion.3
  149.8 1.2 constant_dynamic-slice_fusion.65
  163.3 1.8 constant_dynamic-slice_fusion.47
  199.0 5.5 stack.524
  204.6 6.3 %stack.558 = f32[1,2,33,2080]{3,2,1,0:T(8,128)} concatenate(f32[1,2,1,2080]{3,2,1,0:T(1,128)S(1)} %copy-done.37, f32[1,2,1,2080]{3,2,1,0:T(1,128)} %stack.526, f32[1,2,1,2080]{3,2,1,0:T(1,128)} %stack.527, f32[1,2,1,2080]{3,2,1,0:T(1,128)} %stack.528, f32[1,2,1,2080]{3,2,1,0:T(1,128)S(1)} %copy-done.48, f32[1,2,1,2080]{3,2,1,0:T(1,128)S(1)} %copy-done.49, ...), dimensions={2} | concatenate | bytes 1098240 | tf_op jit(solution)/shard_map/stack | solution.py:68
  211.0 89.0 %all-reduce.4.cloned.1.call-done = f32[1,128,128]{1,2,0:T(8,128)} async-done(((f32[1,128,128]{1,2,0:T(8,128)}), f32[1,128,128]{1,2,0:T(8,128)}) %all-reduce.4.cloned.1.call-update) | async-done | bytes 65552 | tf_op jit(solution)/shard_map/psum | solution.py:60
  299.9 0.9 fusion.66
  301.2 11.9 %custom-call.11 = f32[1,128,128]{2,1,0:T(8,128)S(1)} custom-call(f32[1,128,128]{2,1,0:T(8,128)S(1)} %fusion.46), custom_call_target="Cholesky" | custom-call | tf_op jit(solution)/shard_map/jit(cholesky)/cholesky | solution.py:93
  314.4 9.8 %custom-call.12 = f32[1,1,128,128]{2,3,1,0:T(8,128)S(1)} custom-call(f32[1,1,128,128]{3,2,1,0:T(8,128)S(1)} %fusion.41), custom_call_target="InvertDiagBlocksLowerTriangular" | custom-call | tf_op jit(solution)/shard_map/vmap(jit(_cho_solve))/triangular_solve | solution.py:25
  324.2 58.3 %all-gather.2.cloned.1.call-done = f32[32,1,65,128]{3,1,2,0:T(1,128)} async-done(((f32[1,1,65,128]{3,1,2,0:T(1,128)}), f32[32,1,65,128]{3,1,2,0:T(1,128)}) %all-gather.2.cloned.1.call-update) | async-done | bytes 1064976 | tf_op jit(solution)/shard_map/all_gather | solution.py:59
  382.6 3.1 fusion.9
  386.6 5.1 convolution_bitcast_fusion.1
  391.8 6.0 %copy.575 = f32[1,65,2,2,33,32]{1,5,4,3,2,0:T(8,128)} copy(f32[1,65,2,2,33,32]{4,5,3,2,1,0:T(8,128)} %convolution_bitcast_fusion.1) | data formatting | bytes 2196480 | tf_op jit(solution)/shard_map/fqezc,fbqa->fbezca/transpose | solution.py:105
  397.8 2.6 convolution_bitcast_fusion.2
  402.2 1.3 dynamic-slice.1
  404.1 149.5 %all-reduce.6.cloned.1.call-done = f32[64,1,2,128]{3,0,2,1:T(8,128)} async-done(((f32[64,1,2,128]{3,0,2,1:T(8,128)}), f32[64,1,2,128]{3,0,2,1:T(8,128)}) %all-reduce.6.cloned.1.call-update) | async-done | bytes 65552
  554.3 0.8 copy.577
  555.1 11.8 %all-to-all-start.1 = ((f32[2,1,2,128]{0,2,1,3:T(2,128)}), f32[2,1,2,128]{0,2,1,3:T(2,128)S(1)}, u32[]{:S(2)}, u32[]{:S(2)}) async-start(f32[2,1,2,128]{0,2,1,3:T(2,128)} %copy.577), calls=%async_computation.1 | async-start | bytes 262144 | tf_op jit(solution)/shard_map/all_to_all | solution.py:132
  567.4 8.3 %all-to-all-done.1 = f32[2,1,2,128]{0,2,1,3:T(2,128)S(1)} async-done(((f32[2,1,2,128]{0,2,1,3:T(2,128)}), f32[2,1,2,128]{0,2,1,3:T(2,128)S(1)}, u32[]{:S(2)}, u32[]{:S(2)}) %all-to-all-start.1) | async-done | bytes 2080 | tf_op jit(solution)/shard_map/all_to_all | solution.py:132
  575.9 1.0 convolution_bitcast_fusion
  (402 shorter events, 102.1 us)
Async XLA Ops:
  6.5 136.4 %copy-start = (f32[2,33,64,64]{3,2,1,0:T(8,128)S(1)}, f32[2,33,64,64]{3,2,1,0:T(8,128)}, u32[]{:S(2)}) copy-start(f32[2,33,64,64]{3,2,1,0:T(8,128)} %param.3) | copy-start | bytes 3244036
  9.3 17.6 %all-to-all-start = ((f32[2,8,2,16]{1,0,2,3:T(2,128)}), f32[2,8,2,16]{1,0,2,3:T(2,128)S(1)}, u32[]{:S(2)}, u32[]{:S(2)}) async-start(f32[2,8,2,16]{1,0,2,3:T(2,128)} %copy.367), calls=%async_computation | async-start | bytes 65536 | tf_op jit(solution)/shard_map/all_to_all | solution.py:45
  19.4 280.5 %all-reduce.4.cloned.1.call-start = ((), (), s32[]{:S(2)}) async-start(), calls=%async_computation.3 | async-start | bytes 131072 | tf_op jit(solution)/shard_map/psum | solution.py:60
  113.8 14.5 %copy-start.10 = (f32[1,1,2,33,64]{4,2,3,1,0:T(2,128)S(1)}, f32[1,1,2,33,64]{4,2,3,1,0:T(2,128)}, u32[]{:S(2)}) copy-start(f32[1,1,2,33,64]{4,2,3,1,0:T(2,128)} %get-tuple-element.145) | copy-start | bytes 50692
  114.5 14.5 %copy-start.9 = (f32[1,1,2,33,64]{4,2,3,1,0:T(2,128)S(1)}, f32[1,1,2,33,64]{4,2,3,1,0:T(2,128)}, u32[]{:S(2)}) copy-start(f32[1,1,2,33,64]{4,2,3,1,0:T(2,128)} %get-tuple-element.144) | copy-start | bytes 50692
  115.2 14.6 %copy-start.8 = (f32[1,1,2,33,64]{4,2,3,1,0:T(2,128)S(1)}, f32[1,1,2,33,64]{4,2,3,1,0:T(2,128)}, u32[]{:S(2)}) copy-start(f32[1,1,2,33,64]{4,2,3,1,0:T(2,128)} %get-tuple-element.143) | copy-start | bytes 50692
  115.9 14.5 %copy-start.7 = (f32[1,1,2,33,64]{4,2,3,1,0:T(2,128)S(1)}, f32[1,1,2,33,64]{4,2,3,1,0:T(2,128)}, u32[]{:S(2)}) copy-start(f32[1,1,2,33,64]{4,2,3,1,0:T(2,128)} %get-tuple-element.142) | copy-start | bytes 50692
  116.6 14.5 %copy-start.6 = (f32[1,1,2,33,64]{4,2,3,1,0:T(2,128)S(1)}, f32[1,1,2,33,64]{4,2,3,1,0:T(2,128)}, u32[]{:S(2)}) copy-start(f32[1,1,2,33,64]{4,2,3,1,0:T(2,128)} %get-tuple-element.141) | copy-start | bytes 50692
  117.3 14.5 %copy-start.5 = (f32[1,1,2,33,64]{4,2,3,1,0:T(2,128)S(1)}, f32[1,1,2,33,64]{4,2,3,1,0:T(2,128)}, u32[]{:S(2)}) copy-start(f32[1,1,2,33,64]{4,2,3,1,0:T(2,128)} %get-tuple-element.140) | copy-start | bytes 50692
  118.0 14.6 %copy-start.4 = (f32[1,1,2,33,64]{4,2,3,1,0:T(2,128)S(1)}, f32[1,1,2,33,64]{4,2,3,1,0:T(2,128)}, u32[]{:S(2)}) copy-start(f32[1,1,2,33,64]{4,2,3,1,0:T(2,128)} %get-tuple-element.139) | copy-start | bytes 50692
  118.7 14.5 %copy-start.3 = (f32[1,1,2,33,64]{4,2,3,1,0:T(2,128)S(1)}, f32[1,1,2,33,64]{4,2,3,1,0:T(2,128)}, u32[]{:S(2)}) copy-start(f32[1,1,2,33,64]{4,2,3,1,0:T(2,128)} %get-tuple-element.138) | copy-start | bytes 50692
  119.4 14.6 %copy-start.51 = (f32[2,1,2112]{2,1,0:T(1,128)S(1)}, f32[2,1,2112]{2,1,0:T(1,128)}, u32[]{:S(2)}) copy-start(f32[2,1,2112]{2,1,0:T(1,128)} %stack.571) | copy-start | bytes 50692
  119.4 14.6 %copy-start.52 = (f32[2,1,2112]{2,1,0:T(1,128)S(1)}, f32[2,1,2112]{2,1,0:T(1,128)}, u32[]{:S(2)}) copy-start(f32[2,1,2112]{2,1,0:T(1,128)} %stack.572) | copy-start | bytes 50692
  147.5 235.1 %all-gather.2.cloned.1.call-start = ((), (), s32[]{:S(2)}) async-start(), calls=%async_computation.2 | async-start | bytes 1098240 | tf_op jit(solution)/shard_map/all_gather | solution.py:59
  148.3 405.3 %all-reduce.6.cloned.1.call-start = ((), (), s32[]{:S(2)}) async-start(), calls=%async_computation.4 | async-start | bytes 131072
  188.1 10.6 %copy-start.11 = (f32[1,2,1,2080]{3,2,1,0:T(1,128)S(1)}, f32[1,2,1,2080]{3,2,1,0:T(1,128)}, u32[]{:S(2)}) copy-start(f32[1,2,1,2080]{3,2,1,0:T(1,128)} %stack.491) | copy-start | bytes 49924
  188.1 10.6 %copy-start.12 = (f32[1,2,1,2080]{3,2,1,0:T(1,128)S(1)}, f32[1,2,1,2080]{3,2,1,0:T(1,128)}, u32[]{:S(2)}) copy-start(f32[1,2,1,2080]{3,2,1,0:T(1,128)} %stack.508) | copy-start | bytes 49924
  188.1 10.6 %copy-start.13 = (f32[1,2,1,2080]{3,2,1,0:T(1,128)S(1)}, f32[1,2,1,2080]{3,2,1,0:T(1,128)}, u32[]{:S(2)}) copy-start(f32[1,2,1,2080]{3,2,1,0:T(1,128)} %stack.509) | copy-start | bytes 49924
  188.1 10.6 %copy-start.14 = (f32[1,2,1,2080]{3,2,1,0:T(1,128)S(1)}, f32[1,2,1,2080]{3,2,1,0:T(1,128)}, u32[]{:S(2)}) copy-start(f32[1,2,1,2080]{3,2,1,0:T(1,128)} %stack.510) | copy-start | bytes 49924
  188.2 10.6 %copy-start.15 = (f32[1,2,1,2080]{3,2,1,0:T(1,128)S(1)}, f32[1,2,1,2080]{3,2,1,0:T(1,128)}, u32[]{:S(2)}) copy-start(f32[1,2,1,2080]{3,2,1,0:T(1,128)} %stack.511) | copy-start | bytes 49924
  188.2 10.6 %copy-start.16 = (f32[1,2,1,2080]{3,2,1,0:T(1,128)S(1)}, f32[1,2,1,2080]{3,2,1,0:T(1,128)}, u32[]{:S(2)}) copy-start(f32[1,2,1,2080]{3,2,1,0:T(1,128)} %stack.512) | copy-start | bytes 49924
  188.2 10.6 %copy-start.17 = (f32[1,2,1,2080]{3,2,1,0:T(1,128)S(1)}, f32[1,2,1,2080]{3,2,1,0:T(1,128)}, u32[]{:S(2)}) copy-start(f32[1,2,1,2080]{3,2,1,0:T(1,128)} %stack.513) | copy-start | bytes 49924
  188.2 10.6 %copy-start.18 = (f32[1,2,1,2080]{3,2,1,0:T(1,128)S(1)}, f32[1,2,1,2080]{3,2,1,0:T(1,128)}, u32[]{:S(2)}) copy-start(f32[1,2,1,2080]{3,2,1,0:T(1,128)} %stack.514) | copy-start | bytes 49924
  188.2 10.6 %copy-start.19 = (f32[1,2,1,2080]{3,2,1,0:T(1,128)S(1)}, f32[1,2,1,2080]{3,2,1,0:T(1,128)}, u32[]{:S(2)}) copy-start(f32[1,2,1,2080]{3,2,1,0:T(1,128)} %stack.515) | copy-start | bytes 49924
  188.2 10.6 %copy-start.20 = (f32[1,2,1,2080]{3,2,1,0:T(1,128)S(1)}, f32[1,2,1,2080]{3,2,1,0:T(1,128)}, u32[]{:S(2)}) copy-start(f32[1,2,1,2080]{3,2,1,0:T(1,128)} %stack.516) | copy-start | bytes 49924
  188.2 10.6 %copy-start.21 = (f32[1,2,1,2080]{3,2,1,0:T(1,128)S(1)}, f32[1,2,1,2080]{3,2,1,0:T(1,128)}, u32[]{:S(2)}) copy-start(f32[1,2,1,2080]{3,2,1,0:T(1,128)} %stack.517) | copy-start | bytes 49924
  188.2 10.6 %copy-start.22 = (f32[1,2,1,2080]{3,2,1,0:T(1,128)S(1)}, f32[1,2,1,2080]{3,2,1,0:T(1,128)}, u32[]{:S(2)}) copy-start(f32[1,2,1,2080]{3,2,1,0:T(1,128)} %stack.518) | copy-start | bytes 49924
  188.2 10.6 %copy-start.23 = (f32[1,2,1,2080]{3,2,1,0:T(1,128)S(1)}, f32[1,2,1,2080]{3,2,1,0:T(1,128)}, u32[]{:S(2)}) copy-start(f32[1,2,1,2080]{3,2,1,0:T(1,128)} %stack.519) | copy-start | bytes 49924
  188.2 10.6 %copy-start.24 = (f32[1,2,1,2080]{3,2,1,0:T(1,128)S(1)}, f32[1,2,1,2080]{3,2,1,0:T(1,128)}, u32[]{:S(2)}) copy-start(f32[1,2,1,2080]{3,2,1,0:T(1,128)} %stack.520) | copy-start | bytes 49924
  188.3 10.6 %copy-start.25 = (f32[1,2,1,2080]{3,2,1,0:T(1,128)S(1)}, f32[1,2,1,2080]{3,2,1,0:T(1,128)}, u32[]{:S(2)}) copy-start(f32[1,2,1,2080]{3,2,1,0:T(1,128)} %stack.521) | copy-start | bytes 49924
  188.3 10.6 %copy-start.26 = (f32[1,2,1,2080]{3,2,1,0:T(1,128)S(1)}, f32[1,2,1,2080]{3,2,1,0:T(1,128)}, u32[]{:S(2)}) copy-start(f32[1,2,1,2080]{3,2,1,0:T(1,128)} %stack.522) | copy-start | bytes 49924
  188.3 10.6 %copy-start.27 = (f32[1,2,1,2080]{3,2,1,0:T(1,128)S(1)}, f32[1,2,1,2080]{3,2,1,0:T(1,128)}, u32[]{:S(2)}) copy-start(f32[1,2,1,2080]{3,2,1,0:T(1,128)} %stack.523) | copy-start | bytes 49924
  188.3 10.6 %copy-start.28 = (f32[1,2,1,2080]{3,2,1,0:T(1,128)S(1)}, f32[1,2,1,2080]{3,2,1,0:T(1,128)}, u32[]{:S(2)}) copy-start(f32[1,2,1,2080]{3,2,1,0:T(1,128)} %stack.492) | copy-start | bytes 49924
  188.3 10.6 %copy-start.29 = (f32[1,2,1,2080]{3,2,1,0:T(1,128)S(1)}, f32[1,2,1,2080]{3,2,1,0:T(1,128)}, u32[]{:S(2)}) copy-start(f32[1,2,1,2080]{3,2,1,0:T(1,128)} %stack.493) | copy-start | bytes 49924
  188.3 10.6 %copy-start.30 = (f32[1,2,1,2080]{3,2,1,0:T(1,128)S(1)}, f32[1,2,1,2080]{3,2,1,0:T(1,128)}, u32[]{:S(2)}) copy-start(f32[1,2,1,2080]{3,2,1,0:T(1,128)} %stack.494) | copy-start | bytes 49924
  188.3 10.6 %copy-start.31 = (f32[1,2,1,2080]{3,2,1,0:T(1,128)S(1)}, f32[1,2,1,2080]{3,2,1,0:T(1,128)}, u32[]{:S(2)}) copy-start(f32[1,2,1,2080]{3,2,1,0:T(1,128)} %stack.495) | copy-start | bytes 49924
  188.3 10.6 %copy-start.32 = (f32[1,2,1,2080]{3,2,1,0:T(1,128)S(1)}, f32[1,2,1,2080]{3,2,1,0:T(1,128)}, u32[]{:S(2)}) copy-start(f32[1,2,1,2080]{3,2,1,0:T(1,128)} %stack.496) | copy-start | bytes 49924
  188.3 10.6 %copy-start.33 = (f32[1,2,1,2080]{3,2,1,0:T(1,128)S(1)}, f32[1,2,1,2080]{3,2,1,0:T(1,128)}, u32[]{:S(2)}) copy-start(f32[1,2,1,2080]{3,2,1,0:T(1,128)} %stack.497) | copy-start | bytes 49924
  188.3 10.6 %copy-start.34 = (f32[1,2,1,2080]{3,2,1,0:T(1,128)S(1)}, f32[1,2,1,2080]{3,2,1,0:T(1,128)}, u32[]{:S(2)}) copy-start(f32[1,2,1,2080]{3,2,1,0:T(1,128)} %stack.498) | copy-start | bytes 49924
  188.4 10.6 %copy-start.35 = (f32[1,2,1,2080]{3,2,1,0:T(1,128)S(1)}, f32[1,2,1,2080]{3,2,1,0:T(1,128)}, u32[]{:S(2)}) copy-start(f32[1,2,1,2080]{3,2,1,0:T(1,128)} %stack.499) | copy-start | bytes 49924
  188.4 10.6 %copy-start.36 = (f32[1,2,1,2080]{3,2,1,0:T(1,128)S(1)}, f32[1,2,1,2080]{3,2,1,0:T(1,128)}, u32[]{:S(2)}) copy-start(f32[1,2,1,2080]{3,2,1,0:T(1,128)} %stack.500) | copy-start | bytes 49924
  194.6 10.0 %copy-start.41 = (f32[1,2,1,2080]{3,2,1,0:T(1,128)S(1)}, f32[1,2,1,2080]{3,2,1,0:T(1,128)}, u32[]{:S(2)}) copy-start(f32[1,2,1,2080]{3,2,1,0:T(1,128)} %stack.545) | copy-start | bytes 49924
  194.6 10.0 %copy-start.42 = (f32[1,2,1,2080]{3,2,1,0:T(1,128)S(1)}, f32[1,2,1,2080]{3,2,1,0:T(1,128)}, u32[]{:S(2)}) copy-start(f32[1,2,1,2080]{3,2,1,0:T(1,128)} %stack.546) | copy-start | bytes 49924
  194.6 10.0 %copy-start.43 = (f32[1,2,1,2080]{3,2,1,0:T(1,128)S(1)}, f32[1,2,1,2080]{3,2,1,0:T(1,128)}, u32[]{:S(2)}) copy-start(f32[1,2,1,2080]{3,2,1,0:T(1,128)} %stack.547) | copy-start | bytes 49924
  194.6 10.0 %copy-start.44 = (f32[1,2,1,2080]{3,2,1,0:T(1,128)S(1)}, f32[1,2,1,2080]{3,2,1,0:T(1,128)}, u32[]{:S(2)}) copy-start(f32[1,2,1,2080]{3,2,1,0:T(1,128)} %stack.548) | copy-start | bytes 49924
  194.6 10.0 %copy-start.45 = (f32[1,2,1,2080]{3,2,1,0:T(1,128)S(1)}, f32[1,2,1,2080]{3,2,1,0:T(1,128)}, u32[]{:S(2)}) copy-start(f32[1,2,1,2080]{3,2,1,0:T(1,128)} %stack.549) | copy-start | bytes 49924
  397.8 169.1 %copy-start.54 = (s32[16]{0:T(128)S(1)}, s32[16]{0:T(128)}, u32[]{:S(2)}) copy-start(s32[16]{0:T(128)} %copy-done.53) | copy-start | bytes 196
  555.1 20.7 %all-to-all-start.1 = ((f32[2,1,2,128]{0,2,1,3:T(2,128)}), f32[2,1,2,128]{0,2,1,3:T(2,128)S(1)}, u32[]{:S(2)}, u32[]{:S(2)}) async-start(f32[2,1,2,128]{0,2,1,3:T(2,128)} %copy.577), calls=%async_computation.1 | async-start | bytes 262144 | tf_op jit(solution)/shard_map/all_to_all | solution.py:132
  (14 other events, 99.3 us)
Sparse Core Ops, SparseCore 0:
  147.6 152.2 all-reduce.3
  303.1 79.4 all-gather.1
  402.2 151.3 all-reduce.5
where the time goes:
time: 587 us; the launch traced here: 583 us
  waiting for transfers between devices  313 us (53%)
  local copies, waits for them, and re-layouts  147 us (25%)
  blocking collectives  41.2 us (7%)
  other arithmetic  27.8 us (5%)
  starting transfers between devices  22.2 us (4%)
  matrix products  18.2 us (3%)
  between operations  14.9 us (3%)
    unnamed x4, waiting for transfers between devices  150 us
    psum x1, waiting for transfers between devices, body(): lax.psum(jnp.einsum('afbp,afbq->fpq', own_sketch, own_sketch, precision=h...  89 us
    all_gather x1, waiting for transfers between devices, body(): sketch = lax.all_gather(own_sketch, 'trace', axis=0, tiled=True)  58.3 us
    another operation x66, local copies, waits for them, and re-layouts, body(): jnp.stack([row_slabs[..., anchor:anchor + lag_y] for anchor in range(win_...  53 us
    another operation x68, local copies, waits for them, and re-layouts, body(): jnp.stack([band[:, :, anchor:anchor + win_x] for anchor in range(lag_x)],...  51 us
    all_gather x1, blocking collectives, body(): whole_slices = lax.all_gather(slices, 'trace', axis=2, tiled=True)  41.2 us
    slice x69, local copies, waits for them, and re-layouts, body(): row_slabs[..., anchor:anchor + lag_y]  21.6 us
    another operation x3, other arithmetic, body(): factor = jnp.linalg.cholesky(real_gram)  12.6 us
  transfers between devices with their start and end apart: 5, of which 5 were waited for; matrix products, arithmetic and copies ran while one was open for 15% of the time, Pallas kernels for 0%

commit v1 on v0

--- a/solution.py
+++ b/solution.py
@@ -44,7 +44,9 @@
     spectrum = jnp.einsum("xyt,tpk->xypk", traces.astype(jnp.float32), forward, precision=highest)
     spectrum = lax.all_to_all(spectrum, "freq", split_axis=3, concat_axis=1, tiled=True)
     slices = jnp.transpose(spectrum, (3, 2, 0, 1))
-    whole_slices = lax.all_gather(slices, "trace", axis=2, tiled=True)
+    whole_slices = jnp.concatenate(
+        lax.all_to_all(jnp.stack(lax.axis_size("trace") * [slices]), "trace", 0, 0), 2
+    )
     freq_dev = whole_slices.shape[0]
     first_row = position * own_rows
     row_slabs = jnp.stack([lax.dynamic_slice_in_dim(whole_slices, first_row + 0, lag_x, 2)], axis=1)

time: 587 us -> 561 us (0.956)
  blocking collectives: 41.2 us -> 16.7 us
  waiting for transfers between devices: 313 us -> 295 us
  local copies, waits for them, and re-layouts: 147 us -> 161 us
    all_gather x1 -> x0, blocking collectives: 41.2 us -> none  [body(): whole_slices = lax.all_gather(slices, 'trace', axis=2, tiled=True)]
    another operation x66, local copies, waits for them, and re-layouts: 53 us -> 79.2 us  [body(): jnp.stack([row_slabs[..., anchor:anchor + lag_y] for anchor in range(win_...]
    psum x1, waiting for transfers between devices: 89 us -> 69.7 us  [body(): lax.psum(jnp.einsum('afbp,afbq->fpq', own_sketch, own_sketch, precision=h...]
    slice x69 -> x4, local copies, waits for them, and re-layouts: 21.6 us -> 2.58 us  [body(): row_slabs[..., anchor:anchor + lag_y]]
    all_to_all x0 -> x1, blocking collectives: none -> 16.7 us  [body(): lax.all_to_all(spectrum, 'freq', split_axis=3, concat_axis=1, tiled=True)]
    another operation x68, local copies, waits for them, and re-layouts: 51 us -> 65.9 us  [body(): jnp.stack([band[:, :, anchor:anchor + win_x] for anchor in range(lag_x)],...]
    slice x68 -> x2, local copies, waits for them, and re-layouts: 9.33 us -> 1.47 us  [body(): band[:, :, anchor:anchor + win_x]]
  transfers between devices with their start and end apart: 5 -> 5, of which waited for: 5 -> 5; matrix products, arithmetic and copies ran while one was open for 15% -> 17% of each run, Pallas kernels for 0% -> 0%
where the time goes in v1:
time: 561 us; the launch traced here: 557 us
  waiting for transfers between devices  295 us (53%)
  local copies, waits for them, and re-layouts  161 us (29%)
  other arithmetic  27.7 us (5%)
  starting transfers between devices  24 us (4%)
  matrix products  18.2 us (3%)
  blocking collectives  16.7 us (3%)
  between operations  14.5 us (3%)
    unnamed x4, waiting for transfers between devices  149 us
    another operation x66, local copies, waits for them, and re-layouts, body(): jnp.stack([row_slabs[..., anchor:anchor + lag_y] for anchor in range(win_...  79.2 us
    psum x1, waiting for transfers between devices, body(): lax.psum(jnp.einsum('afbp,afbq->fpq', own_sketch, own_sketch, precision=h...  69.7 us
    another operation x68, local copies, waits for them, and re-layouts, body(): jnp.stack([band[:, :, anchor:anchor + win_x] for anchor in range(lag_x)],...  65.9 us
    all_gather x1, waiting for transfers between devices, body(): sketch = lax.all_gather(own_sketch, 'trace', axis=0, tiled=True)  58.6 us
    all_to_all x1, blocking collectives, body(): lax.all_to_all(spectrum, 'freq', split_axis=3, concat_axis=1, tiled=True)  16.7 us
    another operation x3, other arithmetic, body(): factor = jnp.linalg.cholesky(real_gram)  12.5 us
    all_to_all x1, starting transfers between devices, body(): lax.all_to_all(jnp.stack(lax.axis_size('trace') * [slices]), 'trace', 0, 0)  12 us
  transfers between devices with their start and end apart: 5, of which 5 were waited for; matrix products, arithmetic and copies ran while one was open for 17% of the time, Pallas kernels for 0%

profile of v1, /device:TPU:1, one launch (start us, length us, event | category | flops | bytes accessed | tf_op | source)
XLA Modules:
  0.0 556.7 jit_solution(11808364178098569090)
XLA Ops:
  8.7 16.7 %all_to_all.41 = f32[2,8,2,16]{1,0,2,3:T(2,128)S(1)} all-to-all(f32[2,8,2,16]{1,0,2,3:T(2,128)S(1)} %copy.174), channel_id=1, replica_groups=mesh['freq'=16,'trace'=32] {'freq'}, dimensions={3} | all-to-all | bytes 4096 | tf_op jit(solution)/shard_map/all_to_all | solution.py:45
  26.2 12.0 %all-to-all-start.1 = ((f32[32,1,2,2,128]{4,3,2,1,0:T(2,128)}), f32[32,1,2,2,128]{4,3,2,1,0:T(2,128)S(1)}, u32[]{:S(2)}, u32[]{:S(2)}) async-start(f32[32,1,2,2,128]{4,3,2,1,0:T(2,128)} %stack.459), calls=%async_computation.1 | async-start | bytes 131072 | tf_op jit(solution)/shard_map/all_to_all | solution.py:48
  38.2 8.8 %all-to-all-done.1 = f32[32,1,2,2,128]{4,3,2,1,0:T(2,128)S(1)} async-done(((f32[32,1,2,2,128]{4,3,2,1,0:T(2,128)}), f32[32,1,2,2,128]{4,3,2,1,0:T(2,128)S(1)}, u32[]{:S(2)}, u32[]{:S(2)}) %all-to-all-start.1) | async-done | bytes 65568 | tf_op jit(solution)/shard_map/all_to_all | solution.py:48
  49.6 1.5 stack.606
  51.1 1.5 stack.607
  54.0 1.5 stack.609
  55.5 1.5 stack.610
  59.8 1.5 stack.613
  64.2 1.5 stack.616
  65.7 1.5 stack.617
  67.2 1.5 stack.618
  70.1 1.5 stack.620
  71.5 1.5 stack.621
  73.0 1.5 stack.622
  75.9 1.5 stack.624
  78.9 1.5 stack.626
  81.8 1.5 stack.628
  83.2 1.5 stack.629
  86.2 1.5 stack.631
  87.6 1.5 stack.632
  90.6 1.5 stack.634
  92.0 1.5 stack.635
  93.5 1.5 stack.636
  96.4 1.5 stack.638
  119.8 9.0 %stack.526 = f32[2,65,2112]{2,1,0:T(8,128)S(1)} concatenate(f32[2,1,2112]{2,1,0:T(1,128)} %stack.598, f32[2,1,2112]{2,1,0:T(1,128)} %stack.599, f32[2,1,2112]{2,1,0:T(1,128)} %stack.600, f32[2,1,2112]{2,1,0:T(1,128)} %stack.601, f32[2,1,2112]{2,1,0:T(1,128)} %stack.602, f32[2,1,2112]{2,1,0:T(1,128)} %stack.603, f32[2,1,2112]{2,1,0:T(1,128)} %stack.604, f32[2,1,2112]{2,1,0:T(1,128)} %stack.605, ...), dimensions={1} | concatenate | bytes 2196480 | tf_op jit(solution)/shard_map/stack | solution.py:53
  128.8 3.6 fusion.6
  149.3 1.5 stack.528
  150.8 1.5 stack.529
  152.3 1.5 stack.530
  153.8 1.5 stack.531
  155.2 1.5 stack.532
  156.7 1.5 stack.533
  158.2 1.5 stack.534
  159.6 1.5 stack.535
  161.1 1.5 stack.536
  189.8 7.1 %stack.560 = f32[1,2,33,2080]{3,2,1,0:T(8,128)} concatenate(f32[1,2,1,2080]{3,2,1,0:T(1,128)S(1)} %copy-done.3, f32[1,2,1,2080]{3,2,1,0:T(1,128)S(1)} %copy-done.6, f32[1,2,1,2080]{3,2,1,0:T(1,128)S(1)} %copy-done.7, f32[1,2,1,2080]{3,2,1,0:T(1,128)S(1)} %copy-done.8, f32[1,2,1,2080]{3,2,1,0:T(1,128)S(1)} %copy-done.9, f32[1,2,1,2080]{3,2,1,0:T(1,128)S(1)} %copy-done.10, ...), dimensions={2} | concatenate | bytes 1098240 | tf_op jit(solution)/shard_map/stack | solution.py:70
  197.1 6.3 %stack.594 = f32[1,2,33,2080]{3,2,1,0:T(8,128)} concatenate(f32[1,2,1,2080]{3,2,1,0:T(1,128)} %stack.561, f32[1,2,1,2080]{3,2,1,0:T(1,128)S(1)} %copy-done.34, f32[1,2,1,2080]{3,2,1,0:T(1,128)S(1)} %copy-done.35, f32[1,2,1,2080]{3,2,1,0:T(1,128)S(1)} %copy-done.36, f32[1,2,1,2080]{3,2,1,0:T(1,128)S(1)} %copy-done.37, f32[1,2,1,2080]{3,2,1,0:T(1,128)S(1)} %copy-done.38, ...), dimensions={2} | concatenate | bytes 1098240 | tf_op jit(solution)/shard_map/stack | solution.py:70
  203.5 69.7 %all-reduce.4.cloned.1.call-done = f32[1,128,128]{1,2,0:T(8,128)} async-done(((f32[1,128,128]{1,2,0:T(8,128)}), f32[1,128,128]{1,2,0:T(8,128)}) %all-reduce.4.cloned.1.call-update) | async-done | bytes 65552 | tf_op jit(solution)/shard_map/psum | solution.py:62
  274.3 11.9 %custom-call.11 = f32[1,128,128]{2,1,0:T(8,128)S(1)} custom-call(f32[1,128,128]{2,1,0:T(8,128)S(1)} %fusion.46), custom_call_target="Cholesky" | custom-call | tf_op jit(solution)/shard_map/jit(cholesky)/cholesky | solution.py:95
  287.5 9.8 %custom-call.12 = f32[1,1,128,128]{2,3,1,0:T(8,128)S(1)} custom-call(f32[1,1,128,128]{3,2,1,0:T(8,128)S(1)} %fusion.41), custom_call_target="InvertDiagBlocksLowerTriangular" | custom-call | tf_op jit(solution)/shard_map/vmap(jit(_cho_solve))/triangular_solve | solution.py:25
  297.3 58.6 %all-gather.2.cloned.1.call-done = f32[32,1,65,128]{3,1,2,0:T(1,128)} async-done(((f32[1,1,65,128]{3,1,2,0:T(1,128)}), f32[32,1,65,128]{3,1,2,0:T(1,128)}) %all-gather.2.cloned.1.call-update) | async-done | bytes 1064976 | tf_op jit(solution)/shard_map/all_gather | solution.py:61
  355.9 3.1 fusion.9
  360.0 5.1 convolution_bitcast_fusion.1
  365.1 6.0 %copy.252 = f32[1,65,2,2,33,32]{1,5,4,3,2,0:T(8,128)} copy(f32[1,65,2,2,33,32]{4,5,3,2,1,0:T(8,128)} %convolution_bitcast_fusion.1) | data formatting | bytes 2196480 | tf_op jit(solution)/shard_map/fqezc,fbqa->fbezca/transpose | solution.py:107
  371.1 2.6 convolution_bitcast_fusion.2
  377.4 149.4 %all-reduce.6.cloned.1.call-done = f32[64,1,2,128]{3,0,2,1:T(8,128)} async-done(((f32[64,1,2,128]{3,0,2,1:T(8,128)}), f32[64,1,2,128]{3,0,2,1:T(8,128)}) %all-reduce.6.cloned.1.call-update) | async-done | bytes 65552
  528.4 11.8 %all-to-all-start.2 = ((f32[2,1,2,128]{0,2,1,3:T(2,128)}), f32[2,1,2,128]{0,2,1,3:T(2,128)S(1)}, u32[]{:S(2)}, u32[]{:S(2)}) async-start(f32[2,1,2,128]{0,2,1,3:T(2,128)} %copy.254), calls=%async_computation.2 | async-start | bytes 262144 | tf_op jit(solution)/shard_map/all_to_all | solution.py:134
  540.8 8.3 %all-to-all-done.2 = f32[2,1,2,128]{0,2,1,3:T(2,128)S(1)} async-done(((f32[2,1,2,128]{0,2,1,3:T(2,128)}), f32[2,1,2,128]{0,2,1,3:T(2,128)S(1)}, u32[]{:S(2)}, u32[]{:S(2)}) %all-to-all-start.2) | async-done | bytes 2080 | tf_op jit(solution)/shard_map/all_to_all | solution.py:134
  (258 shorter events, 98.6 us)
Async XLA Ops:
  6.5 122.3 %copy-start = (f32[2,33,64,64]{3,2,1,0:T(8,128)S(1)}, f32[2,33,64,64]{3,2,1,0:T(8,128)}, u32[]{:S(2)}) copy-start(f32[2,33,64,64]{3,2,1,0:T(8,128)} %param.3) | copy-start | bytes 3244036
  26.2 20.8 %all-to-all-start.1 = ((f32[32,1,2,2,128]{4,3,2,1,0:T(2,128)}), f32[32,1,2,2,128]{4,3,2,1,0:T(2,128)S(1)}, u32[]{:S(2)}, u32[]{:S(2)}) async-start(f32[32,1,2,2,128]{4,3,2,1,0:T(2,128)} %stack.459), calls=%async_computation.1 | async-start | bytes 131072 | tf_op jit(solution)/shard_map/all_to_all | solution.py:48
  38.1 235.0 %all-reduce.4.cloned.1.call-start = ((), (), s32[]{:S(2)}) async-start(), calls=%async_computation.4 | async-start | bytes 131072 | tf_op jit(solution)/shard_map/psum | solution.py:62
  98.6 21.3 %copy-start.43 = (f32[2,1,2112]{2,1,0:T(1,128)S(1)}, f32[2,1,2112]{2,1,0:T(1,128)}, u32[]{:S(2)}) copy-start(f32[2,1,2112]{2,1,0:T(1,128)} %stack.606) | copy-start | bytes 50692
  98.6 21.3 %copy-start.44 = (f32[2,1,2112]{2,1,0:T(1,128)S(1)}, f32[2,1,2112]{2,1,0:T(1,128)}, u32[]{:S(2)}) copy-start(f32[2,1,2112]{2,1,0:T(1,128)} %stack.607) | copy-start | bytes 50692
  133.4 222.5 %all-gather.2.cloned.1.call-start = ((), (), s32[]{:S(2)}) async-start(), calls=%async_computation.3 | async-start | bytes 1098240 | tf_op jit(solution)/shard_map/all_gather | solution.py:61
  134.2 392.7 %all-reduce.6.cloned.1.call-start = ((), (), s32[]{:S(2)}) async-start(), calls=%async_computation.5 | async-start | bytes 131072
  149.3 40.3 %copy-start.3 = (f32[1,2,1,2080]{3,2,1,0:T(1,128)S(1)}, f32[1,2,1,2080]{3,2,1,0:T(1,128)}, u32[]{:S(2)}) copy-start(f32[1,2,1,2080]{3,2,1,0:T(1,128)} %stack.527) | copy-start | bytes 49924
  149.3 40.3 %copy-start.4 = (f32[1,2,1,2080]{3,2,1,0:T(1,128)S(1)}, f32[1,2,1,2080]{3,2,1,0:T(1,128)}, u32[]{:S(2)}) copy-start(f32[1,2,1,2080]{3,2,1,0:T(1,128)} %stack.544) | copy-start | bytes 49924
  149.3 40.3 %copy-start.5 = (f32[1,2,1,2080]{3,2,1,0:T(1,128)S(1)}, f32[1,2,1,2080]{3,2,1,0:T(1,128)}, u32[]{:S(2)}) copy-start(f32[1,2,1,2080]{3,2,1,0:T(1,128)} %stack.545) | copy-start | bytes 49924
  163.3 26.3 %copy-start.6 = (f32[1,2,1,2080]{3,2,1,0:T(1,128)S(1)}, f32[1,2,1,2080]{3,2,1,0:T(1,128)}, u32[]{:S(2)}) copy-start(f32[1,2,1,2080]{3,2,1,0:T(1,128)} %stack.528) | copy-start | bytes 49924
  163.3 26.3 %copy-start.7 = (f32[1,2,1,2080]{3,2,1,0:T(1,128)S(1)}, f32[1,2,1,2080]{3,2,1,0:T(1,128)}, u32[]{:S(2)}) copy-start(f32[1,2,1,2080]{3,2,1,0:T(1,128)} %stack.529) | copy-start | bytes 49924
  164.0 25.6 %copy-start.8 = (f32[1,2,1,2080]{3,2,1,0:T(1,128)S(1)}, f32[1,2,1,2080]{3,2,1,0:T(1,128)}, u32[]{:S(2)}) copy-start(f32[1,2,1,2080]{3,2,1,0:T(1,128)} %stack.530) | copy-start | bytes 49924
  164.7 24.9 %copy-start.9 = (f32[1,2,1,2080]{3,2,1,0:T(1,128)S(1)}, f32[1,2,1,2080]{3,2,1,0:T(1,128)}, u32[]{:S(2)}) copy-start(f32[1,2,1,2080]{3,2,1,0:T(1,128)} %stack.531) | copy-start | bytes 49924
  165.5 24.2 %copy-start.10 = (f32[1,2,1,2080]{3,2,1,0:T(1,128)S(1)}, f32[1,2,1,2080]{3,2,1,0:T(1,128)}, u32[]{:S(2)}) copy-start(f32[1,2,1,2080]{3,2,1,0:T(1,128)} %stack.532) | copy-start | bytes 49924
  166.2 23.5 %copy-start.11 = (f32[1,2,1,2080]{3,2,1,0:T(1,128)S(1)}, f32[1,2,1,2080]{3,2,1,0:T(1,128)}, u32[]{:S(2)}) copy-start(f32[1,2,1,2080]{3,2,1,0:T(1,128)} %stack.533) | copy-start | bytes 49924
  166.9 22.8 %copy-start.12 = (f32[1,2,1,2080]{3,2,1,0:T(1,128)S(1)}, f32[1,2,1,2080]{3,2,1,0:T(1,128)}, u32[]{:S(2)}) copy-start(f32[1,2,1,2080]{3,2,1,0:T(1,128)} %stack.534) | copy-start | bytes 49924
  167.6 22.1 %copy-start.13 = (f32[1,2,1,2080]{3,2,1,0:T(1,128)S(1)}, f32[1,2,1,2080]{3,2,1,0:T(1,128)}, u32[]{:S(2)}) copy-start(f32[1,2,1,2080]{3,2,1,0:T(1,128)} %stack.535) | copy-start | bytes 49924
  168.3 21.4 %copy-start.14 = (f32[1,2,1,2080]{3,2,1,0:T(1,128)S(1)}, f32[1,2,1,2080]{3,2,1,0:T(1,128)}, u32[]{:S(2)}) copy-start(f32[1,2,1,2080]{3,2,1,0:T(1,128)} %stack.536) | copy-start | bytes 49924
  169.1 20.6 %copy-start.15 = (f32[1,2,1,2080]{3,2,1,0:T(1,128)S(1)}, f32[1,2,1,2080]{3,2,1,0:T(1,128)}, u32[]{:S(2)}) copy-start(f32[1,2,1,2080]{3,2,1,0:T(1,128)} %stack.537) | copy-start | bytes 49924
  169.8 19.9 %copy-start.16 = (f32[1,2,1,2080]{3,2,1,0:T(1,128)S(1)}, f32[1,2,1,2080]{3,2,1,0:T(1,128)}, u32[]{:S(2)}) copy-start(f32[1,2,1,2080]{3,2,1,0:T(1,128)} %stack.538) | copy-start | bytes 49924
  170.5 19.2 %copy-start.17 = (f32[1,2,1,2080]{3,2,1,0:T(1,128)S(1)}, f32[1,2,1,2080]{3,2,1,0:T(1,128)}, u32[]{:S(2)}) copy-start(f32[1,2,1,2080]{3,2,1,0:T(1,128)} %stack.539) | copy-start | bytes 49924
  171.2 18.5 %copy-start.18 = (f32[1,2,1,2080]{3,2,1,0:T(1,128)S(1)}, f32[1,2,1,2080]{3,2,1,0:T(1,128)}, u32[]{:S(2)}) copy-start(f32[1,2,1,2080]{3,2,1,0:T(1,128)} %stack.540) | copy-start | bytes 49924
  172.0 17.8 %copy-start.19 = (f32[1,2,1,2080]{3,2,1,0:T(1,128)S(1)}, f32[1,2,1,2080]{3,2,1,0:T(1,128)}, u32[]{:S(2)}) copy-start(f32[1,2,1,2080]{3,2,1,0:T(1,128)} %stack.541) | copy-start | bytes 49924
  172.7 24.2 %copy-start.20 = (f32[1,2,1,2080]{3,2,1,0:T(1,128)S(1)}, f32[1,2,1,2080]{3,2,1,0:T(1,128)}, u32[]{:S(2)}) copy-start(f32[1,2,1,2080]{3,2,1,0:T(1,128)} %stack.580) | copy-start | bytes 49924
  173.4 23.5 %copy-start.21 = (f32[1,2,1,2080]{3,2,1,0:T(1,128)S(1)}, f32[1,2,1,2080]{3,2,1,0:T(1,128)}, u32[]{:S(2)}) copy-start(f32[1,2,1,2080]{3,2,1,0:T(1,128)} %stack.581) | copy-start | bytes 49924
  174.1 22.8 %copy-start.22 = (f32[1,2,1,2080]{3,2,1,0:T(1,128)S(1)}, f32[1,2,1,2080]{3,2,1,0:T(1,128)}, u32[]{:S(2)}) copy-start(f32[1,2,1,2080]{3,2,1,0:T(1,128)} %stack.582) | copy-start | bytes 49924
  174.8 22.1 %copy-start.23 = (f32[1,2,1,2080]{3,2,1,0:T(1,128)S(1)}, f32[1,2,1,2080]{3,2,1,0:T(1,128)}, u32[]{:S(2)}) copy-start(f32[1,2,1,2080]{3,2,1,0:T(1,128)} %stack.583) | copy-start | bytes 49924
  175.6 21.4 %copy-start.24 = (f32[1,2,1,2080]{3,2,1,0:T(1,128)S(1)}, f32[1,2,1,2080]{3,2,1,0:T(1,128)}, u32[]{:S(2)}) copy-start(f32[1,2,1,2080]{3,2,1,0:T(1,128)} %stack.584) | copy-start | bytes 49924
  176.3 20.7 %copy-start.25 = (f32[1,2,1,2080]{3,2,1,0:T(1,128)S(1)}, f32[1,2,1,2080]{3,2,1,0:T(1,128)}, u32[]{:S(2)}) copy-start(f32[1,2,1,2080]{3,2,1,0:T(1,128)} %stack.585) | copy-start | bytes 49924
  177.0 20.0 %copy-start.26 = (f32[1,2,1,2080]{3,2,1,0:T(1,128)S(1)}, f32[1,2,1,2080]{3,2,1,0:T(1,128)}, u32[]{:S(2)}) copy-start(f32[1,2,1,2080]{3,2,1,0:T(1,128)} %stack.586) | copy-start | bytes 49924
  177.7 19.3 %copy-start.27 = (f32[1,2,1,2080]{3,2,1,0:T(1,128)S(1)}, f32[1,2,1,2080]{3,2,1,0:T(1,128)}, u32[]{:S(2)}) copy-start(f32[1,2,1,2080]{3,2,1,0:T(1,128)} %stack.587) | copy-start | bytes 49924
  178.4 18.5 %copy-start.28 = (f32[1,2,1,2080]{3,2,1,0:T(1,128)S(1)}, f32[1,2,1,2080]{3,2,1,0:T(1,128)}, u32[]{:S(2)}) copy-start(f32[1,2,1,2080]{3,2,1,0:T(1,128)} %stack.588) | copy-start | bytes 49924
  179.1 17.8 %copy-start.29 = (f32[1,2,1,2080]{3,2,1,0:T(1,128)S(1)}, f32[1,2,1,2080]{3,2,1,0:T(1,128)}, u32[]{:S(2)}) copy-start(f32[1,2,1,2080]{3,2,1,0:T(1,128)} %stack.589) | copy-start | bytes 49924
  179.9 17.1 %copy-start.30 = (f32[1,2,1,2080]{3,2,1,0:T(1,128)S(1)}, f32[1,2,1,2080]{3,2,1,0:T(1,128)}, u32[]{:S(2)}) copy-start(f32[1,2,1,2080]{3,2,1,0:T(1,128)} %stack.590) | copy-start | bytes 49924
  180.6 16.4 %copy-start.31 = (f32[1,2,1,2080]{3,2,1,0:T(1,128)S(1)}, f32[1,2,1,2080]{3,2,1,0:T(1,128)}, u32[]{:S(2)}) copy-start(f32[1,2,1,2080]{3,2,1,0:T(1,128)} %stack.591) | copy-start | bytes 49924
  181.3 15.7 %copy-start.32 = (f32[1,2,1,2080]{3,2,1,0:T(1,128)S(1)}, f32[1,2,1,2080]{3,2,1,0:T(1,128)}, u32[]{:S(2)}) copy-start(f32[1,2,1,2080]{3,2,1,0:T(1,128)} %stack.592) | copy-start | bytes 49924
  182.0 15.0 %copy-start.33 = (f32[1,2,1,2080]{3,2,1,0:T(1,128)S(1)}, f32[1,2,1,2080]{3,2,1,0:T(1,128)}, u32[]{:S(2)}) copy-start(f32[1,2,1,2080]{3,2,1,0:T(1,128)} %stack.593) | copy-start | bytes 49924
  182.8 14.3 %copy-start.34 = (f32[1,2,1,2080]{3,2,1,0:T(1,128)S(1)}, f32[1,2,1,2080]{3,2,1,0:T(1,128)}, u32[]{:S(2)}) copy-start(f32[1,2,1,2080]{3,2,1,0:T(1,128)} %stack.562) | copy-start | bytes 49924
  183.5 13.6 %copy-start.35 = (f32[1,2,1,2080]{3,2,1,0:T(1,128)S(1)}, f32[1,2,1,2080]{3,2,1,0:T(1,128)}, u32[]{:S(2)}) copy-start(f32[1,2,1,2080]{3,2,1,0:T(1,128)} %stack.563) | copy-start | bytes 49924
  184.2 12.8 %copy-start.36 = (f32[1,2,1,2080]{3,2,1,0:T(1,128)S(1)}, f32[1,2,1,2080]{3,2,1,0:T(1,128)}, u32[]{:S(2)}) copy-start(f32[1,2,1,2080]{3,2,1,0:T(1,128)} %stack.564) | copy-start | bytes 49924
  184.9 12.1 %copy-start.37 = (f32[1,2,1,2080]{3,2,1,0:T(1,128)S(1)}, f32[1,2,1,2080]{3,2,1,0:T(1,128)}, u32[]{:S(2)}) copy-start(f32[1,2,1,2080]{3,2,1,0:T(1,128)} %stack.565) | copy-start | bytes 49924
  185.6 11.4 %copy-start.38 = (f32[1,2,1,2080]{3,2,1,0:T(1,128)S(1)}, f32[1,2,1,2080]{3,2,1,0:T(1,128)}, u32[]{:S(2)}) copy-start(f32[1,2,1,2080]{3,2,1,0:T(1,128)} %stack.566) | copy-start | bytes 49924
  186.4 10.7 %copy-start.39 = (f32[1,2,1,2080]{3,2,1,0:T(1,128)S(1)}, f32[1,2,1,2080]{3,2,1,0:T(1,128)}, u32[]{:S(2)}) copy-start(f32[1,2,1,2080]{3,2,1,0:T(1,128)} %stack.567) | copy-start | bytes 49924
  187.1 10.0 %copy-start.40 = (f32[1,2,1,2080]{3,2,1,0:T(1,128)S(1)}, f32[1,2,1,2080]{3,2,1,0:T(1,128)}, u32[]{:S(2)}) copy-start(f32[1,2,1,2080]{3,2,1,0:T(1,128)} %stack.568) | copy-start | bytes 49924
  187.8 9.3 %copy-start.41 = (f32[1,2,1,2080]{3,2,1,0:T(1,128)S(1)}, f32[1,2,1,2080]{3,2,1,0:T(1,128)}, u32[]{:S(2)}) copy-start(f32[1,2,1,2080]{3,2,1,0:T(1,128)} %stack.569) | copy-start | bytes 49924
  371.1 169.1 %copy-start.46 = (s32[16]{0:T(128)S(1)}, s32[16]{0:T(128)}, u32[]{:S(2)}) copy-start(s32[16]{0:T(128)} %copy-done.45) | copy-start | bytes 196
  528.4 20.7 %all-to-all-start.2 = ((f32[2,1,2,128]{0,2,1,3:T(2,128)}), f32[2,1,2,128]{0,2,1,3:T(2,128)S(1)}, u32[]{:S(2)}, u32[]{:S(2)}) async-start(f32[2,1,2,128]{0,2,1,3:T(2,128)} %copy.254), calls=%async_computation.2 | async-start | bytes 262144 | tf_op jit(solution)/shard_map/all_to_all | solution.py:134
  (6 other events, 22.5 us)
Sparse Core Ops, SparseCore 0:
  133.5 139.5 all-reduce.3
  276.3 79.5 all-gather.1
  375.5 151.3 all-reduce.5
